TPU v7x, 256 devices: a whole 4x4x8 slice. The times are simulated.
256 devices in a mesh: fsdp: 64 (over x_lo, z, y), dp: 4 (over x_hi, core).
Axes of the slice: x: 4 (x_hi: 2, x_lo: 2; x = x_hi * 2 + x_lo), y: 4, z: 8, core: 2. Of those that a mesh axis runs over, the one named last changes fastest.
Arguments:
- tokens: bfloat16 [4, 8192, 8192], P('dp', 'fsdp'), may hold values from -6 to 6
- queries: bfloat16 [4, 8192, 4096], P('dp', 'fsdp'), may hold values from -40 to 40, as said below
- keys: bfloat16 [4, 8192, 512], P('dp', 'fsdp'), may hold values from -4 to 4
- memory: bfloat16 [4, 8192, 8192], P('dp', 'fsdp'), may hold values from -6 to 6
- mem_keys: bfloat16 [4, 8192, 512], P('dp', 'fsdp'), may hold values from -4 to 4
- cotangent: bfloat16 [4, 8192, 4096], P('dp', 'fsdp'), may hold values from -6 to 6
- value_weight: bfloat16 [8192, 512], P('fsdp'), may hold values from -0.0625 to 0.0625
- dest_group: int32 [4, 128], P('dp', 'fsdp'), may hold values from 0 to 3, as said below
- source_group: int32 [4, 128], P('dp', 'fsdp'), may hold values from 0 to 3, as said below
- lengths: int32 [4, 128], P('dp', 'fsdp'), may hold values from 1 to 64
Outputs:
- grad_queries: bfloat16 [4, 8192, 4096], P('dp', 'fsdp')
- grad_keys: bfloat16 [4, 8192, 512], P('dp', 'fsdp')
- grad_memory: bfloat16 [4, 8192, 8192], P('dp', 'fsdp')
- grad_mem_keys: bfloat16 [4, 8192, 512], P('dp', 'fsdp')
- grad_weight: bfloat16 [8192, 512], P('fsdp')
Inputs may be any that keep to these rules, and one draw needn't show every extreme that they name: `queries`: large in the hidden draw where a query row copies its own key. `dest_group`: the 2 documents of a device go to two different groups, never its own; document k of every device of one fsdp index moves the same number of groups ahead. `source_group`: consistent with dest_group: every device receives exactly one document for each of its slots, at most one from each sender.
All inputs are finite; a program needn't handle non-finite values.
Results may differ from a plain program's by a relative error of at most 0.0075.
Values may be sent and summed in bfloat16 or wider, within the bound.
No kernel may reach another device: no remote copies, remote signals or barrier semaphores. Data moves between devices by JAX's collectives and lax.ppermute only.
A program may use at most 128 MiB of HBM per device.

v0:
```python
import jax
import jax.numpy as jnp
from jax import lax
from jax.sharding import PartitionSpec as P

HEAD_DIM = 128


def attend(query_rows, seg_keys, seg_values, slot_keys, slot_values, upstream, length):
    seg_len = query_rows.shape[0]
    mem_len = slot_keys.shape[0]
    kv_width = seg_keys.shape[1]
    heads_kv = kv_width // HEAD_DIM
    group_size = query_rows.shape[1] // kv_width
    key_count = seg_len + mem_len
    all_keys = jnp.concatenate([slot_keys, seg_keys], axis=0).reshape(key_count, heads_kv, HEAD_DIM)
    all_values = jnp.concatenate([slot_values, seg_values], axis=0).reshape(
        key_count, heads_kv, HEAD_DIM
    )
    query_heads = query_rows.reshape(seg_len, heads_kv, group_size, HEAD_DIM)
    score_scale = HEAD_DIM ** (-0.5)
    scores = (
        jnp.einsum("qkgd,jkd->kgqj", query_heads, all_keys, preferred_element_type=jnp.float32)
        * score_scale
    )
    positions = jnp.arange(seg_len)[:, None]
    columns = jnp.arange(key_count)[None, :]
    visible = (columns < mem_len) | (columns - mem_len <= positions)
    scores = jnp.where(visible, scores, -1e30)
    row_max = jnp.max(scores, axis=-1, keepdims=True)
    exp_scores = jnp.exp(scores - row_max)
    weights = exp_scores / jnp.sum(exp_scores, axis=-1, keepdims=True)
    weights_low = weights.astype(jnp.bfloat16)
    output = jnp.einsum(
        "kgqj,jkd->qkgd", weights_low, all_values, preferred_element_type=jnp.float32
    ).astype(jnp.bfloat16)
    live_rows = (jnp.arange(seg_len) < length).astype(jnp.bfloat16)
    masked = (
        upstream.reshape(seg_len, heads_kv, group_size, HEAD_DIM) * live_rows[:, None, None, None]
    )
    grad_weights = jnp.einsum(
        "qkgd,jkd->kgqj", masked, all_values, preferred_element_type=jnp.float32
    )
    grad_values = jnp.einsum(
        "kgqj,qkgd->jkd", weights_low, masked, preferred_element_type=jnp.float32
    ).reshape(key_count, kv_width)
    row_delta = jnp.einsum("qkgd,qkgd->kgq", masked, output, preferred_element_type=jnp.float32)
    grad_scores = (weights * (grad_weights - row_delta[..., None]) * score_scale).astype(
        jnp.bfloat16
    )
    grad_query = (
        jnp.einsum("kgqj,jkd->qkgd", grad_scores, all_keys, preferred_element_type=jnp.float32)
        .reshape(seg_len, -1)
        .astype(jnp.bfloat16)
    )
    grad_all_keys = jnp.einsum(
        "kgqj,qkgd->jkd", grad_scores, query_heads, preferred_element_type=jnp.float32
    ).reshape(key_count, kv_width)
    return (
        grad_query,
        grad_all_keys[:mem_len],
        grad_all_keys[mem_len:],
        grad_values[:mem_len],
        grad_values[mem_len:],
    )


def per_device(
    tokens,
    queries,
    keys,
    memory,
    mem_keys,
    cotangent,
    value_weight,
    dest_group,
    source_group,
    lengths,
):
    groups = lax.axis_size("dp")
    slot_count = dest_group.shape[1]
    seg_len = tokens.shape[1] // slot_count
    mem_len = memory.shape[1] // slot_count
    kv_width = value_weight.shape[1]
    model_width = tokens.shape[2]
    weight_full = lax.all_gather(value_weight, "fsdp", axis=0, tiled=True)
    stacked = jnp.concatenate([tokens[0], memory[0]], axis=0)
    values = jnp.dot(stacked, weight_full, preferred_element_type=jnp.float32).astype(jnp.bfloat16)
    split_at = slot_count * seg_len
    seg_values = values[:split_at].reshape(slot_count, seg_len, kv_width)
    doc_values = values[split_at:].reshape(slot_count, mem_len, kv_width)
    doc_keys = mem_keys[0].reshape(slot_count, mem_len, kv_width)
    targets = jnp.arange(groups, dtype=jnp.int32)
    send_table = (dest_group[0][None, :] == targets[:, None]).astype(jnp.bfloat16)
    take_table = (source_group[0][:, None] == targets[None, :]).astype(jnp.bfloat16)
    out_keys = jnp.einsum(
        "hs,smc->hmc", send_table, doc_keys, preferred_element_type=jnp.float32
    ).astype(jnp.bfloat16)
    out_values = jnp.einsum(
        "hs,smc->hmc", send_table, doc_values, preferred_element_type=jnp.float32
    ).astype(jnp.bfloat16)
    in_keys, in_values = (
        lax.all_to_all(out_keys, "dp", split_axis=0, concat_axis=0, tiled=True),
        lax.all_to_all(out_values, "dp", split_axis=0, concat_axis=0, tiled=True),
    )
    slot_keys = jnp.einsum(
        "sh,hmc->smc", take_table, in_keys, preferred_element_type=jnp.float32
    ).astype(jnp.bfloat16)
    slot_values = jnp.einsum(
        "sh,hmc->smc", take_table, in_values, preferred_element_type=jnp.float32
    ).astype(jnp.bfloat16)
    query_slots = queries[0].reshape(slot_count, seg_len, -1)
    key_slots = keys[0].reshape(slot_count, seg_len, kv_width)
    upstream_slots = cotangent[0].reshape(slot_count, seg_len, -1)
    grad_query, slot_grad_keys, seg_grad_keys, slot_grad_values, seg_grad_values = jax.vmap(attend)(
        query_slots, key_slots, seg_values, slot_keys, slot_values, upstream_slots, lengths[0]
    )
    back_keys = jnp.einsum(
        "sh,smc->hmc",
        take_table,
        slot_grad_keys.astype(jnp.bfloat16),
        preferred_element_type=jnp.float32,
    ).astype(jnp.bfloat16)
    back_values = jnp.einsum(
        "sh,smc->hmc",
        take_table,
        slot_grad_values.astype(jnp.bfloat16),
        preferred_element_type=jnp.float32,
    ).astype(jnp.bfloat16)
    ret_keys, ret_values = (
        lax.all_to_all(back_keys, "dp", split_axis=0, concat_axis=0, tiled=True),
        lax.all_to_all(back_values, "dp", split_axis=0, concat_axis=0, tiled=True),
    )
    doc_grad_keys = jnp.einsum(
        "hs,hmc->smc", send_table, ret_keys, preferred_element_type=jnp.float32
    ).astype(jnp.bfloat16)
    doc_grad_values = jnp.einsum(
        "hs,hmc->smc", send_table, ret_values, preferred_element_type=jnp.float32
    ).astype(jnp.bfloat16)
    doc_grad_flat = doc_grad_values.reshape(slot_count * mem_len, kv_width)
    grad_memory = lax.dot_general(
        doc_grad_flat, weight_full, (((1,), (1,)), ((), ())), preferred_element_type=jnp.float32
    ).astype(jnp.bfloat16)
    value_grads_all = jnp.concatenate(
        [seg_grad_values.astype(jnp.bfloat16).reshape(-1, kv_width), doc_grad_flat], axis=0
    )
    shares = lax.psum_scatter(
        lax.dot_general(
            stacked, value_grads_all, (((0,), (0,)), ((), ())), preferred_element_type=jnp.float32
        ),
        "fsdp",
        scatter_dimension=0,
        tiled=True,
    )
    grad_weight = lax.psum(shares, "dp").astype(jnp.bfloat16)
    return (
        grad_query.reshape(1, slot_count * seg_len, -1),
        seg_grad_keys.astype(jnp.bfloat16).reshape(1, slot_count * seg_len, kv_width),
        grad_memory.reshape(1, slot_count * mem_len, model_width),
        doc_grad_keys.reshape(1, slot_count * mem_len, kv_width),
        grad_weight,
    )


def solution(mesh):
    in_specs = (
        P("dp", "fsdp", None),
        P("dp", "fsdp", None),
        P("dp", "fsdp", None),
        P("dp", "fsdp", None),
        P("dp", "fsdp", None),
        P("dp", "fsdp", None),
        P("fsdp", None),
        P("dp", "fsdp"),
        P("dp", "fsdp"),
        P("dp", "fsdp"),
    )
    out_specs = (
        P("dp", "fsdp", None),
        P("dp", "fsdp", None),
        P("dp", "fsdp", None),
        P("dp", "fsdp", None),
        P("fsdp", None),
    )
    return jax.shard_map(
        per_device, mesh=mesh, in_specs=in_specs, out_specs=out_specs, check_vma=False
    )
```

profile of v0, /device:TPU:1, one launch (start us, length us, event | category | flops | bytes accessed | tf_op | source)
XLA Modules:
  0.0 706.9 jit_solution(6315596288376271972)
XLA Ops:
  8.1 1.1 convolution_convert_fusion.6
  10.0 7.2 %all-to-all-start = ((bf16[4,64,512]{2,1,0:T(8,128)(2,1)}), bf16[4,64,512]{2,1,0:T(8,128)(2,1)}, u32[]{:S(2)}, u32[]{:S(2)}) async-start(bf16[4,64,512]{2,1,0:T(8,128)(2,1)} %copy.35), calls=%async_computation | async-start | bytes 524288 | tf_op jit(solution)/shard_map/all_to_all | solution.py:103
  18.9 4.9 all-to-all-done
  23.8 1.3 convolution_convert_fusion.10
  25.3 2.3 fusion.70
  27.6 2.0 fusion.22
  31.4 1.1 copy.69
  33.6 5.0 all-to-all-start.2
  38.6 1.1 copy.71
  39.7 5.6 all-to-all-done.2
  45.3 1.3 convolution_convert_fusion.8
  46.6 10.4 %fusion.3 = f32[8192,512]{1,0:T(8,128)} fusion(bf16[128,8192]{1,0:T(8,128)(2,1)} %bitcast.133, bf16[128,8192]{1,0:T(8,128)(2,1)} %bitcast.135, bf16[128,512]{1,0:T(8,128)(2,1)S(1)} %bitcast.137, bf16[128,512]{1,0:T(8,128)(2,1)S(1)} %bitcast.145), kind=kOutput, calls=%fused_computation.5 | convolution fusion | flops 2156396544 | bytes 21233664 | tf_op jit(solution)/shard_map/dot_general | solution.py:148
  57.0 225.1 %all-gather.2.cloned.1.call-done = bf16[8192,512]{1,0:T(8,128)(2,1)} async-done(((bf16[128,512]{1,0:T(8,128)(2,1)}), bf16[8192,512]{1,0:T(8,128)(2,1)}) %all-gather.2.cloned.1.call-update) | async-done | bytes 8388624 | tf_op jit(solution)/shard_map/all_gather | solution.py:86
  282.1 7.0 fusion.14
  290.9 46.7 %all-to-all-start.1 = ((bf16[4,64,512]{2,1,0:T(8,128)(2,1)}), bf16[4,64,512]{2,1,0:T(8,128)(2,1)}, u32[]{:S(2)}, u32[]{:S(2)}) async-start(bf16[4,64,512]{2,1,0:T(8,128)(2,1)} %copy.41), calls=%async_computation.1 | async-start | bytes 524288 | tf_op jit(solution)/shard_map/all_to_all | solution.py:104
  337.6 7.5 %fusion.2 = bf16[1,128,8192]{2,1,0:T(8,128)(2,1)} fusion(bf16[128,512]{1,0:T(8,128)(2,1)S(1)} %bitcast.138, bf16[8192,512]{1,0:T(8,128)(2,1)} %all-gather.2.cloned.1.call-done), kind=kOutput, calls=%fused_computation.3 | convolution fusion | flops 1074790400 | bytes 10616832 | tf_op jit(solution)/shard_map/dot_general | solution.py:141
  346.1 1.3 convolution_convert_fusion.9
  349.1 2.2 fusion
  351.3 2.7 fusion.7
  356.3 4.8 all-to-all-start.3
  362.2 1.3 convert_element_type.86
  364.2 3.5 all-to-all-done.3
  368.7 264.8 %reduce-scatter.2.cloned.1.call-done = f32[128,512]{1,0:T(8,128)} async-done(((f32[8192,512]{1,0:T(8,128)}), f32[128,512]{1,0:T(8,128)}) %reduce-scatter.2.cloned.1.call-update) | async-done | bytes 262160 | tf_op jit(solution)/shard_map/reduce_scatter | solution.py:147
  633.5 66.5 %all-reduce.1 = bf16[128,512]{1,0:T(8,128)(2,1)} all-reduce(f32[128,512]{1,0:T(8,128)} %reduce-scatter.2.cloned.1.call-done), channel_id=1, replica_groups=mesh['fsdp'=64,'dp'=4] {'dp'}, use_global_device_ids=true, to_apply=%region_3.4 | all-reduce | flops 65536 | bytes 393216 | tf_op jit(solution)/shard_map/psum | solution.py:155
  (60 shorter events, 16.0 us)
Async XLA Ops:
  7.2 0.9 copy-start
  7.2 11.0 %copy-start.1 = (bf16[1,128,4096]{2,1,0:T(8,128)(2,1)S(1)}, bf16[1,128,4096]{2,1,0:T(8,128)(2,1)}, u32[]{:S(2)}) copy-start(bf16[1,128,4096]{2,1,0:T(8,128)(2,1)} %param.11) | copy-start | bytes 3145732
  7.2 274.9 %all-gather.2.cloned.1.call-start = ((), (), s32[]{:S(2)}) async-start(), calls=%async_computation.5 | async-start | bytes 8519680 | tf_op jit(solution)/shard_map/all_gather | solution.py:86
  8.1 10.4 %copy-start.2 = (bf16[1,128,4096]{2,1,0:T(8,128)(2,1)S(1)}, bf16[1,128,4096]{2,1,0:T(8,128)(2,1)}, u32[]{:S(2)}) copy-start(bf16[1,128,4096]{2,1,0:T(8,128)(2,1)} %param.15) | copy-start | bytes 3145732
  10.0 13.8 %all-to-all-start = ((bf16[4,64,512]{2,1,0:T(8,128)(2,1)}), bf16[4,64,512]{2,1,0:T(8,128)(2,1)}, u32[]{:S(2)}, u32[]{:S(2)}) async-start(bf16[4,64,512]{2,1,0:T(8,128)(2,1)} %copy.35), calls=%async_computation | async-start | bytes 524288 | tf_op jit(solution)/shard_map/all_to_all | solution.py:103
  18.1 7.1 %copy-start.3 = (bf16[2,64,4,128]{3,1,2,0:T(8,128)(2,1)}, bf16[2,64,4,128]{3,1,2,0:T(8,128)(2,1)S(1)}, u32[]{:S(2)}) copy-start(bf16[2,64,4,128]{3,1,2,0:T(8,128)(2,1)S(1)} %copy.38) | copy-start | bytes 393220
  18.2 0.7 copy-start.8
  18.2 5.7 copy-start.9
  25.3 2.3 copy-start.5
  27.6 2.9 copy-start.7
  30.5 14.8 %copy-start.10 = (s32[1,2]{1,0:T(1,128)S(1)}, s32[1,2]{1,0:T(1,128)}, u32[]{:S(2)}) copy-start(s32[1,2]{1,0:T(1,128)} %param.17) | copy-start | bytes 28
  33.6 11.6 %all-to-all-start.2 = ((bf16[4,64,512]{2,1,0:T(8,128)(2,1)}), bf16[4,64,512]{2,1,0:T(8,128)(2,1)}, u32[]{:S(2)}, u32[]{:S(2)}) async-start(bf16[4,64,512]{2,1,0:T(8,128)(2,1)} %copy.50), calls=%async_computation.2 | async-start | bytes 524288 | tf_op jit(solution)/shard_map/all_to_all | solution.py:132
  38.6 594.9 %reduce-scatter.2.cloned.1.call-start = ((), (), s32[]{:S(2)}) async-start(), calls=%async_computation.6 | async-start | bytes 17039360 | tf_op jit(solution)/shard_map/reduce_scatter | solution.py:147
  290.9 55.2 %all-to-all-start.1 = ((bf16[4,64,512]{2,1,0:T(8,128)(2,1)}), bf16[4,64,512]{2,1,0:T(8,128)(2,1)}, u32[]{:S(2)}, u32[]{:S(2)}) async-start(bf16[4,64,512]{2,1,0:T(8,128)(2,1)} %copy.41), calls=%async_computation.1 | async-start | bytes 524288 | tf_op jit(solution)/shard_map/all_to_all | solution.py:104
  354.8 6.3 copy-start.4
  354.8 6.3 copy-start.6
  356.3 11.4 %all-to-all-start.3 = ((bf16[4,64,512]{2,1,0:T(8,128)(2,1)}), bf16[4,64,512]{2,1,0:T(8,128)(2,1)S(1)}, u32[]{:S(2)}, u32[]{:S(2)}) async-start(bf16[4,64,512]{2,1,0:T(8,128)(2,1)} %copy.54), calls=%async_computation.3 | async-start | bytes 524288 | tf_op jit(solution)/shard_map/all_to_all | solution.py:131
Sparse Core Ops, SparseCore 0:
  9.8 272.2 all-gather.1
  284.6 348.8 reduce-scatter.1
where the time goes:
time: 708 us; the launch traced here: 707 us
  waiting for transfers between devices  505 us (71%)
  blocking collectives  66.5 us (9%)
  starting transfers between devices  63.7 us (9%)
  matrix products  40.8 us (6%)
  local copies, waits for them, and re-layouts  14.9 us (2%)
  between operations  14.4 us (2%)
    reduce_scatter x1, waiting for transfers between devices, per_device(): lax.psum_scatter(lax.dot_general(stacked, value_grads_all, (((0,), (0,)),...  265 us
    all_gather x1, waiting for transfers between devices, per_device(): weight_full = lax.all_gather(value_weight, 'fsdp', axis=0, tiled=True)  225 us
    psum x1, blocking collectives, per_device(): grad_weight = lax.psum(shares, 'dp').astype(jnp.bfloat16)  66.5 us
    all_to_all x1, starting transfers between devices, per_device(): lax.all_to_all(out_values, 'dp', split_axis=0, concat_axis=0, tiled=True)  46.7 us
  transfers between devices with their start and end apart: 6, of which 5 were waited for; matrix products, arithmetic and copies ran while one was open for 8% of the time, Pallas kernels for 0%

commit v1 on v0

--- a/solution.py
+++ b/solution.py
@@ -2,6 +2,7 @@
 import jax.numpy as jnp
 from jax import lax
 from jax.sharding import PartitionSpec as P
+from jax.lax import all_to_all, axis_size
 
 HEAD_DIM = 128
 
@@ -83,7 +84,9 @@
     mem_len = memory.shape[1] // slot_count
     kv_width = value_weight.shape[1]
     model_width = tokens.shape[2]
-    weight_full = lax.all_gather(value_weight, "fsdp", axis=0, tiled=True)
+    weight_full = jnp.concatenate(
+        all_to_all(jnp.stack(axis_size("fsdp") * [value_weight]), "fsdp", 0, 0), axis=0
+    )
     stacked = jnp.concatenate([tokens[0], memory[0]], axis=0)
     values = jnp.dot(stacked, weight_full, preferred_element_type=jnp.float32).astype(jnp.bfloat16)
     split_at = slot_count * seg_len

time: 708 us -> 546 us (0.77)
  waiting for transfers between devices: 505 us -> 142 us
  blocking collectives: 66.5 us -> 317 us
  starting transfers between devices: 63.7 us -> 22.9 us
    all_to_all x0 -> x1, blocking collectives: none -> 272 us  [per_device(): all_to_all(jnp.stack(axis_size('fsdp') * [value_weight]), 'fsdp', 0, 0)]
    all_gather x1 -> x0, waiting for transfers between devices: 225 us -> none  [per_device(): weight_full = lax.all_gather(value_weight, 'fsdp', axis=0, tiled=True)]
    reduce_scatter x1, waiting for transfers between devices: 265 us -> 127 us  [per_device(): lax.psum_scatter(lax.dot_general(stacked, value_grads_all, (((0,), (0,)),...]
    all_to_all x1, starting transfers between devices: 46.7 us -> 6.56 us  [per_device(): lax.all_to_all(out_values, 'dp', split_axis=0, concat_axis=0, tiled=True)]
    psum x1, blocking collectives: 66.5 us -> 45.2 us  [per_device(): grad_weight = lax.psum(shares, 'dp').astype(jnp.bfloat16)]
  transfers between devices with their start and end apart: 6 -> 5, of which waited for: 5 -> 4; matrix products, arithmetic and copies ran while one was open for 8% -> 5% of each run, Pallas kernels for 0% -> 0%
where the time goes in v1:
time: 546 us; the launch traced here: 545 us
  blocking collectives  317 us (58%)
  waiting for transfers between devices  142 us (26%)
  matrix products  34.2 us (6%)
  starting transfers between devices  22.9 us (4%)
  between operations  14.4 us (3%)
  local copies, waits for them, and re-layouts  12 us (2%)
    all_to_all x1, blocking collectives, per_device(): all_to_all(jnp.stack(axis_size('fsdp') * [value_weight]), 'fsdp', 0, 0)  272 us
    reduce_scatter x1, waiting for transfers between devices, per_device(): lax.psum_scatter(lax.dot_general(stacked, value_grads_all, (((0,), (0,)),...  127 us
    psum x1, blocking collectives, per_device(): grad_weight = lax.psum(shares, 'dp').astype(jnp.bfloat16)  45.2 us
  transfers between devices with their start and end apart: 5, of which 4 were waited for; matrix products, arithmetic and copies ran while one was open for 5% of the time, Pallas kernels for 0%

profile of v1, /device:TPU:1, one launch (start us, length us, event | category | flops | bytes accessed | tf_op | source)
XLA Modules:
  0.0 544.5 jit_solution(8620923027837767879)
XLA Ops:
  8.1 1.1 convolution_convert_fusion.6
  9.9 7.2 %all-to-all-start = ((bf16[4,64,512]{2,1,0:T(8,128)(2,1)}), bf16[4,64,512]{2,1,0:T(8,128)(2,1)}, u32[]{:S(2)}, u32[]{:S(2)}) async-start(bf16[4,64,512]{2,1,0:T(8,128)(2,1)} %copy.35), calls=%async_computation | async-start | bytes 524288 | tf_op jit(solution)/shard_map/all_to_all | solution.py:106
  18.2 5.6 %all-to-all-done = bf16[4,64,512]{2,1,0:T(8,128)(2,1)} async-done(((bf16[4,64,512]{2,1,0:T(8,128)(2,1)}), bf16[4,64,512]{2,1,0:T(8,128)(2,1)}, u32[]{:S(2)}, u32[]{:S(2)}) %all-to-all-start) | async-done | bytes 262176 | tf_op jit(solution)/shard_map/all_to_all | solution.py:106
  23.7 1.3 convolution_convert_fusion.10
  25.2 2.3 fusion.70
  27.5 1.9 fusion.22
  29.4 0.9 fusion.13
  31.8 4.3 all-to-all-start.3
  36.3 6.4 %all-to-all-done.3 = bf16[4,64,512]{2,1,0:T(8,128)(2,1)S(1)} async-done(((bf16[4,64,512]{2,1,0:T(8,128)(2,1)}), bf16[4,64,512]{2,1,0:T(8,128)(2,1)S(1)}, u32[]{:S(2)}, u32[]{:S(2)}) %all-to-all-start.3) | async-done | bytes 262176 | tf_op jit(solution)/shard_map/all_to_all | solution.py:135
  43.1 10.3 %fusion.3 = f32[8192,512]{1,0:T(8,128)} fusion(bf16[128,8192]{1,0:T(8,128)(2,1)} %bitcast.136, bf16[128,8192]{1,0:T(8,128)(2,1)} %bitcast.138, bf16[128,512]{1,0:T(8,128)(2,1)S(1)} %bitcast.140, bf16[128,512]{1,0:T(8,128)(2,1)S(1)} %bitcast.148), kind=kOutput, calls=%fused_computation.5 | convolution fusion | flops 2156396544 | bytes 21233664 | tf_op jit(solution)/shard_map/dot_general | solution.py:151
  53.5 0.9 copy-done.8
  54.4 1.0 stack.2
  55.4 271.7 %all_to_all.25 = bf16[64,128,512]{2,1,0:T(8,128)(2,1)S(1)} all-to-all(bf16[64,128,512]{2,1,0:T(8,128)(2,1)S(1)} %stack.2), channel_id=1, replica_groups=mesh['fsdp'=64,'dp'=4] {'fsdp'}, dimensions={0} | all-to-all | bytes 16777216 | tf_op jit(solution)/shard_map/all_to_all | solution.py:88
  327.1 2.3 fusion.14
  329.5 0.9 copy-done.1
  331.5 6.6 %all-to-all-start.2 = ((bf16[4,64,512]{2,1,0:T(8,128)(2,1)}), bf16[4,64,512]{2,1,0:T(8,128)(2,1)S(1)}, u32[]{:S(2)}, u32[]{:S(2)}) async-start(bf16[4,64,512]{2,1,0:T(8,128)(2,1)} %copy.41), calls=%async_computation.2 | async-start | bytes 524288 | tf_op jit(solution)/shard_map/all_to_all | solution.py:107
  338.1 7.6 %fusion.2 = bf16[1,128,8192]{2,1,0:T(8,128)(2,1)} fusion(bf16[128,512]{1,0:T(8,128)(2,1)S(1)} %bitcast.141, bf16[8192,512]{1,0:T(8,128)(2,1)} %bitcast.132), kind=kOutput, calls=%fused_computation.3 | convolution fusion | flops 1074790400 | bytes 10616832 | tf_op jit(solution)/shard_map/dot_general | solution.py:144
  346.2 2.2 fusion
  348.4 2.8 fusion.7
  353.4 4.7 all-to-all-start.4
  359.3 1.3 convert_element_type.86
  361.4 3.5 all-to-all-done.4
  365.9 126.7 %reduce-scatter.2.cloned.1.call-done = f32[128,512]{1,0:T(8,128)} async-done(((f32[8192,512]{1,0:T(8,128)}), f32[128,512]{1,0:T(8,128)}) %reduce-scatter.2.cloned.1.call-update) | async-done | bytes 262160 | tf_op jit(solution)/shard_map/reduce_scatter | solution.py:150
  492.5 45.2 %all-reduce.1 = bf16[128,512]{1,0:T(8,128)(2,1)} all-reduce(f32[128,512]{1,0:T(8,128)} %reduce-scatter.2.cloned.1.call-done), channel_id=1, replica_groups=mesh['fsdp'=64,'dp'=4] {'dp'}, use_global_device_ids=true, to_apply=%region_3.4 | all-reduce | flops 65536 | bytes 393216 | tf_op jit(solution)/shard_map/psum | solution.py:158
  (63 shorter events, 11.6 us)
Async XLA Ops:
  7.2 0.9 copy-start
  7.2 9.9 %copy-start.4 = (bf16[1,128,4096]{2,1,0:T(8,128)(2,1)S(1)}, bf16[1,128,4096]{2,1,0:T(8,128)(2,1)}, u32[]{:S(2)}) copy-start(bf16[1,128,4096]{2,1,0:T(8,128)(2,1)} %param.15) | copy-start | bytes 3145732
  7.2 10.2 %copy-start.5 = (bf16[1,128,4096]{2,1,0:T(8,128)(2,1)S(1)}, bf16[1,128,4096]{2,1,0:T(8,128)(2,1)}, u32[]{:S(2)}) copy-start(bf16[1,128,4096]{2,1,0:T(8,128)(2,1)} %param.11) | copy-start | bytes 3145732
  9.9 13.9 %all-to-all-start = ((bf16[4,64,512]{2,1,0:T(8,128)(2,1)}), bf16[4,64,512]{2,1,0:T(8,128)(2,1)}, u32[]{:S(2)}, u32[]{:S(2)}) async-start(bf16[4,64,512]{2,1,0:T(8,128)(2,1)} %copy.35), calls=%async_computation | async-start | bytes 524288 | tf_op jit(solution)/shard_map/all_to_all | solution.py:106
  17.1 0.9 copy-start.9
  17.1 1.0 copy-start.10
  17.1 6.6 %copy-start.11 = (s32[1,2]{1,0:T(1,128)S(1)}, s32[1,2]{1,0:T(1,128)}, u32[]{:S(2)}) copy-start(s32[1,2]{1,0:T(1,128)} %param.18) | copy-start | bytes 28
  18.0 9.5 %copy-start.6 = (bf16[16,8,32,128]{3,2,1,0:T(8,128)(2,1)}, bf16[16,8,32,128]{3,2,1,0:T(8,128)(2,1)S(1)}, u32[]{:S(2)}) copy-start(bf16[16,8,32,128]{3,2,1,0:T(8,128)(2,1)S(1)} %copy.72) | copy-start | bytes 3145732
  30.4 12.4 %copy-start.12 = (s32[1,2]{1,0:T(1,128)S(1)}, s32[1,2]{1,0:T(1,128)}, u32[]{:S(2)}) copy-start(s32[1,2]{1,0:T(1,128)} %param.17) | copy-start | bytes 28
  31.8 10.9 %all-to-all-start.3 = ((bf16[4,64,512]{2,1,0:T(8,128)(2,1)}), bf16[4,64,512]{2,1,0:T(8,128)(2,1)S(1)}, u32[]{:S(2)}, u32[]{:S(2)}) async-start(bf16[4,64,512]{2,1,0:T(8,128)(2,1)} %copy.50), calls=%async_computation.3 | async-start | bytes 524288 | tf_op jit(solution)/shard_map/all_to_all | solution.py:135
  36.2 456.3 %reduce-scatter.2.cloned.1.call-start = ((), (), s32[]{:S(2)}) async-start(), calls=%async_computation.6 | async-start | bytes 17039360 | tf_op jit(solution)/shard_map/reduce_scatter | solution.py:150
  53.5 0.9 copy-start.8
  55.4 271.8 %copy-start.2 = (bf16[1,128,8192]{2,1,0:T(8,128)(2,1)S(1)}, bf16[1,128,8192]{2,1,0:T(8,128)(2,1)}, u32[]{:S(2)}) copy-start(bf16[1,128,8192]{2,1,0:T(8,128)(2,1)} %param.13) | copy-start | bytes 6291460
  55.4 271.8 %copy-start.3 = (bf16[1,128,8192]{2,1,0:T(8,128)(2,1)S(1)}, bf16[1,128,8192]{2,1,0:T(8,128)(2,1)}, u32[]{:S(2)}) copy-start(bf16[1,128,8192]{2,1,0:T(8,128)(2,1)} %param.10) | copy-start | bytes 6291460
  327.1 3.2 copy-start.1
  331.5 14.2 %all-to-all-start.2 = ((bf16[4,64,512]{2,1,0:T(8,128)(2,1)}), bf16[4,64,512]{2,1,0:T(8,128)(2,1)S(1)}, u32[]{:S(2)}, u32[]{:S(2)}) async-start(bf16[4,64,512]{2,1,0:T(8,128)(2,1)} %copy.41), calls=%async_computation.2 | async-start | bytes 524288 | tf_op jit(solution)/shard_map/all_to_all | solution.py:107
  348.4 2.8 copy-start.7
  353.4 11.4 %all-to-all-start.4 = ((bf16[4,64,512]{2,1,0:T(8,128)(2,1)}), bf16[4,64,512]{2,1,0:T(8,128)(2,1)S(1)}, u32[]{:S(2)}, u32[]{:S(2)}) async-start(bf16[4,64,512]{2,1,0:T(8,128)(2,1)} %copy.54), calls=%async_computation.4 | async-start | bytes 524288 | tf_op jit(solution)/shard_map/all_to_all | solution.py:134
Sparse Core Ops, SparseCore 0:
  53.6 438.8 reduce-scatter.1
